TPU v7x, 32 devices: a whole 2x2x4 slice. The times are simulated.
32 devices in a mesh: ctx: 8 (over z, y), tp: 4 (over x, core).
Axes of the slice: x: 2, y: 2, z: 4, core: 2. Of those that a mesh axis runs over, the one named last changes fastest.
Arguments:
- queries: bfloat16 [2048, 16, 128], P('ctx', 'tp'), may hold values from -12 to 12
- keys: bfloat16 [2048, 8, 128], P('ctx', 'tp'), may hold values from -6 to 6
- values: bfloat16 [2048, 8, 128], P('ctx', 'tp'), may hold values from -6 to 6
- residual: bfloat16 [2048, 3072], P('ctx', 'tp'), may hold values from -6 to 6
- out_weight: bfloat16 [16, 128, 3072], P(None, None, 'tp'), may hold values from -1 to 1
- post_gain: bfloat16 [3072], P('tp'), may hold values from 0.099609375 to 1.8984375
Outputs:
- mixed: bfloat16 [2048, 3072], P('ctx', 'tp')
All inputs are finite; a program needn't handle non-finite values.
Results may differ from a plain program's by a relative error of at most 0.015.
Values may be sent and summed in bfloat16 or wider, within the bound.
No kernel may reach another device: no remote copies, remote signals or barrier semaphores. Data moves between devices by JAX's collectives and lax.ppermute only.
A program may use at most 64 MiB of HBM per device.

v0:
```python
import jax
import jax.numpy as jnp
from jax import lax
from jax.sharding import PartitionSpec as P

WINDOW_TOKENS = 4096
D = 3072
softcap_value = 50.0
query_scale = 1.0 / 12.0
rope_base = 10000.0


def passed_along(value, axis, steps):
    count = lax.axis_size(axis)
    first, last = (max(0, -steps), min(count, count - steps))
    return lax.ppermute(value, axis, [(source, source + steps) for source in range(first, last)])


def rotate(values_in, positions):
    half_width = values_in.shape[-1] // 2
    steps_half = jnp.arange(half_width, dtype=jnp.float32)
    inverse = rope_base ** (-2.0 * steps_half / values_in.shape[-1])
    angles = positions.astype(jnp.float32)[..., None] * inverse
    cosine = jnp.cos(angles)
    sine_part = jnp.sin(angles)
    first_half = values_in[..., :half_width]
    second_half = values_in[..., half_width:]
    return jnp.concatenate(
        [
            first_half * cosine - second_half * sine_part,
            second_half * cosine + first_half * sine_part,
        ],
        axis=-1,
    )


def attend_block(state, key_block, value_block, source, rotary_queries, device_index):
    numerators, denominators = state
    rows = key_block.shape[0]
    scores = (
        jnp.einsum("sgrh,kgh->grsk", rotary_queries, key_block, preferred_element_type=jnp.float32)
        * query_scale
    )
    capped = softcap_value * jnp.tanh(scores / softcap_value)
    offsets = jnp.arange(rows, dtype=jnp.int32)
    query_pos = device_index * rows + offsets
    key_pos = source * rows + offsets
    distance = query_pos[:, None] - key_pos[None, :]
    allowed = (distance >= 0) & (distance < WINDOW_TOKENS) & (key_pos[None, :] >= 0)
    weights = jnp.where(allowed[None, None], jnp.exp(capped), 0.0)
    denominators = denominators + jnp.sum(weights, axis=-1)
    numerators = numerators + jnp.einsum(
        "grsk,kgh->grsh",
        weights.astype(jnp.bfloat16),
        value_block,
        preferred_element_type=jnp.float32,
    )
    return (numerators, denominators)


def local(queries, keys, values, residual, out_weight, post_gain):
    rows = queries.shape[0]
    q_heads = queries.shape[1]
    head_size = queries.shape[2]
    kv_heads = keys.shape[1]
    heads_per_group = q_heads // kv_heads
    cycle_size = lax.axis_size("ctx")
    device_index = lax.axis_index("ctx")
    positions = (device_index * rows + jnp.arange(rows, dtype=jnp.int32))[:, None]
    rotary_queries = rotate(queries.astype(jnp.float32), positions).astype(jnp.bfloat16)
    rotary_queries = rotary_queries.reshape(rows, kv_heads, heads_per_group, head_size)
    rotary_keys = rotate(keys.astype(jnp.float32), positions).astype(jnp.bfloat16)
    reach = min(WINDOW_TOKENS // rows, cycle_size - 1)
    state = (
        jnp.zeros((kv_heads, heads_per_group, rows, head_size), jnp.float32),
        jnp.zeros((kv_heads, heads_per_group, rows), jnp.float32),
    )
    state = attend_block(state, rotary_keys, values, device_index, rotary_queries, device_index)

    def advance(step_index, carried):
        running, key_block, value_block = carried
        key_block, value_block = passed_along((key_block, value_block), "ctx", 1)
        running = attend_block(
            running,
            key_block,
            value_block,
            device_index - step_index - 1,
            rotary_queries,
            device_index,
        )
        return (running, key_block, value_block)

    state, unused_keys, unused_values = lax.fori_loop(
        0, reach, advance, (state, rotary_keys, values)
    )
    numerators, denominators = state
    attended = (numerators / denominators[..., None]).astype(jnp.bfloat16)
    attended = jnp.transpose(attended, (2, 0, 1, 3)).reshape(rows, q_heads, head_size)
    local_cols = out_weight.shape[2]
    piece = lax.all_gather(attended, "tp", axis=1, tiled=True)
    heads_in = piece.shape[1]
    weight_rows = out_weight.reshape(heads_in * head_size, local_cols)
    projected = jnp.dot(
        piece.reshape(rows, heads_in * head_size), weight_rows, preferred_element_type=jnp.float32
    )
    square_sums = lax.psum(jnp.sum(projected * projected, axis=1), "tp")
    normed = projected * lax.rsqrt(square_sums / D + 1e-06)[:, None] * post_gain.astype(jnp.float32)
    mixed = residual.astype(jnp.float32) + normed
    return mixed.astype(jnp.bfloat16)


def solution(mesh):
    in_specs = (
        P("ctx", "tp", None),
        P("ctx", "tp", None),
        P("ctx", "tp", None),
        P("ctx", "tp"),
        P(None, None, "tp"),
        P("tp"),
    )
    out_specs = P("ctx", "tp")
    return jax.shard_map(local, mesh=mesh, in_specs=in_specs, out_specs=out_specs, check_vma=False)
```

profile of v0, /device:TPU:0, one launch (start us, length us, event | category | flops | bytes accessed | tf_op | source)
XLA Modules:
  0.0 137.2 jit_solution(11933492602181658960)
XLA Ops:
  16.1 85.1 %while.21 = (s32[]{:T(128)}, f32[2,2,256,128]{3,2,1,0:T(8,128)}, f32[2,2,256]{2,1,0:T(2,128)S(1)}, bf16[256,2,128]{2,0,1:T(8,128)(2,1)}, bf16[256,2,128]{2,0,1:T...) while((s32[]{:T(128)}, f32[2,2,256,128]{3,2,1,0:T(8,128)}, ...), condition=%wide.region_3.4_spmd, body=%wide.region_1.3_spmd.sunk | while | flops 135988224 | bytes 8540965 | solution.py:93
  16.1 4.9 %collective-permute-start = (bf16[256,2,128]{2,0,1:T(8,128)(2,1)}, bf16[256,2,128]{2,0,1:T(8,128)(2,1)S(1)}, u32[]{:S(2)}, u32[]{:S(2)}) collective-permute-start(bf16[256,2,128]{2,0,1:T(8,128)(2,1)} %get-tuple-element.308), channel_id=1, source_target_pairs={{0,4},{4,8},{8,12},{12,16},{16,20},{20,24},{24,28},{1,5},{5,9},{9,... | collective-permute-start | bytes 393224 | tf_op jit(solution)/shard_map/while/body/eval_jaxpr/ppermute | solution.py:16
  21.0 3.4 %collective-permute-start.1 = (bf16[256,2,128]{2,0,1:T(8,128)(2,1)S(1)}, bf16[256,2,128]{2,0,1:T(8,128)(2,1)S(1)}, u32[]{:S(2)}, u32[]{:S(2)}) collective-permute-start(bf16[256,2,128]{2,0,1:T(8,128)(2,1)S(1)} %get-tuple-element.309), channel_id=1, source_target_pairs={{0,4},{4,8},{8,12},{12,16},{16,20},{20,24},{24,28},{1,5},{5,9},{9,... | collective-permute-start | bytes 393224 | tf_op jit(solution)/shard_map/while/body/eval_jaxpr/ppermute | solution.py:16
  24.7 1.4 %fusion.40 = (f32[2,2,256]{2,1,0:T(2,128)S(1)}, bf16[2,2,256,256]{2,3,1,0:T(8,128)(2,1)S(1)}) fusion(bf16[256,2,2,128]{3,0,2,1:T(8,128)(2,1)} %get-tuple-element.323, bf16[256,2,128]{2,0,1:T(8,128)(2,1)S(1)} %collective-permute-done, pred[256,256]{0,1:T(8,128)(4,1)S(1)} %fusion.39), kind=kOutput, calls=%fused_computation.49.clone.1 | convolution fusion | flops 68418560 | bytes 987136 | tf_op jit(solution)/shard_map/while/body/eval_jaxpr/sgrh,kgh->grsk/dot_general | solution.py:41
  28.2 4.3 %collective-permute-start = (bf16[256,2,128]{2,0,1:T(8,128)(2,1)}, bf16[256,2,128]{2,0,1:T(8,128)(2,1)S(1)}, u32[]{:S(2)}, u32[]{:S(2)}) collective-permute-start(bf16[256,2,128]{2,0,1:T(8,128)(2,1)} %get-tuple-element.308), channel_id=1, source_target_pairs={{0,4},{4,8},{8,12},{12,16},{16,20},{20,24},{24,28},{1,5},{5,9},{9,... | collective-permute-start | bytes 393224 | tf_op jit(solution)/shard_map/while/body/eval_jaxpr/ppermute | solution.py:16
  32.5 4.3 %collective-permute-start.1 = (bf16[256,2,128]{2,0,1:T(8,128)(2,1)S(1)}, bf16[256,2,128]{2,0,1:T(8,128)(2,1)S(1)}, u32[]{:S(2)}, u32[]{:S(2)}) collective-permute-start(bf16[256,2,128]{2,0,1:T(8,128)(2,1)S(1)} %get-tuple-element.309), channel_id=1, source_target_pairs={{0,4},{4,8},{8,12},{12,16},{16,20},{20,24},{24,28},{1,5},{5,9},{9,... | collective-permute-start | bytes 393224 | tf_op jit(solution)/shard_map/while/body/eval_jaxpr/ppermute | solution.py:16
  40.6 4.3 %collective-permute-start = (bf16[256,2,128]{2,0,1:T(8,128)(2,1)}, bf16[256,2,128]{2,0,1:T(8,128)(2,1)S(1)}, u32[]{:S(2)}, u32[]{:S(2)}) collective-permute-start(bf16[256,2,128]{2,0,1:T(8,128)(2,1)} %get-tuple-element.308), channel_id=1, source_target_pairs={{0,4},{4,8},{8,12},{12,16},{16,20},{20,24},{24,28},{1,5},{5,9},{9,... | collective-permute-start | bytes 393224 | tf_op jit(solution)/shard_map/while/body/eval_jaxpr/ppermute | solution.py:16
  45.0 4.1 %collective-permute-start.1 = (bf16[256,2,128]{2,0,1:T(8,128)(2,1)S(1)}, bf16[256,2,128]{2,0,1:T(8,128)(2,1)S(1)}, u32[]{:S(2)}, u32[]{:S(2)}) collective-permute-start(bf16[256,2,128]{2,0,1:T(8,128)(2,1)S(1)} %get-tuple-element.309), channel_id=1, source_target_pairs={{0,4},{4,8},{8,12},{12,16},{16,20},{20,24},{24,28},{1,5},{5,9},{9,... | collective-permute-start | bytes 393224 | tf_op jit(solution)/shard_map/while/body/eval_jaxpr/ppermute | solution.py:16
  52.8 4.4 %collective-permute-start = (bf16[256,2,128]{2,0,1:T(8,128)(2,1)}, bf16[256,2,128]{2,0,1:T(8,128)(2,1)S(1)}, u32[]{:S(2)}, u32[]{:S(2)}) collective-permute-start(bf16[256,2,128]{2,0,1:T(8,128)(2,1)} %get-tuple-element.308), channel_id=1, source_target_pairs={{0,4},{4,8},{8,12},{12,16},{16,20},{20,24},{24,28},{1,5},{5,9},{9,... | collective-permute-start | bytes 393224 | tf_op jit(solution)/shard_map/while/body/eval_jaxpr/ppermute | solution.py:16
  57.2 3.7 %collective-permute-start.1 = (bf16[256,2,128]{2,0,1:T(8,128)(2,1)S(1)}, bf16[256,2,128]{2,0,1:T(8,128)(2,1)S(1)}, u32[]{:S(2)}, u32[]{:S(2)}) collective-permute-start(bf16[256,2,128]{2,0,1:T(8,128)(2,1)S(1)} %get-tuple-element.309), channel_id=1, source_target_pairs={{0,4},{4,8},{8,12},{12,16},{16,20},{20,24},{24,28},{1,5},{5,9},{9,... | collective-permute-start | bytes 393224 | tf_op jit(solution)/shard_map/while/body/eval_jaxpr/ppermute | solution.py:16
  61.1 1.4 %fusion.40 = (f32[2,2,256]{2,1,0:T(2,128)S(1)}, bf16[2,2,256,256]{2,3,1,0:T(8,128)(2,1)S(1)}) fusion(bf16[256,2,2,128]{3,0,2,1:T(8,128)(2,1)} %get-tuple-element.323, bf16[256,2,128]{2,0,1:T(8,128)(2,1)S(1)} %collective-permute-done, pred[256,256]{0,1:T(8,128)(4,1)S(1)} %fusion.39), kind=kOutput, calls=%fused_computation.49.clone.1 | convolution fusion | flops 68418560 | bytes 987136 | tf_op jit(solution)/shard_map/while/body/eval_jaxpr/sgrh,kgh->grsk/dot_general | solution.py:41
  64.6 4.3 %collective-permute-start = (bf16[256,2,128]{2,0,1:T(8,128)(2,1)}, bf16[256,2,128]{2,0,1:T(8,128)(2,1)S(1)}, u32[]{:S(2)}, u32[]{:S(2)}) collective-permute-start(bf16[256,2,128]{2,0,1:T(8,128)(2,1)} %get-tuple-element.308), channel_id=1, source_target_pairs={{0,4},{4,8},{8,12},{12,16},{16,20},{20,24},{24,28},{1,5},{5,9},{9,... | collective-permute-start | bytes 393224 | tf_op jit(solution)/shard_map/while/body/eval_jaxpr/ppermute | solution.py:16
  69.0 4.1 %collective-permute-start.1 = (bf16[256,2,128]{2,0,1:T(8,128)(2,1)S(1)}, bf16[256,2,128]{2,0,1:T(8,128)(2,1)S(1)}, u32[]{:S(2)}, u32[]{:S(2)}) collective-permute-start(bf16[256,2,128]{2,0,1:T(8,128)(2,1)S(1)} %get-tuple-element.309), channel_id=1, source_target_pairs={{0,4},{4,8},{8,12},{12,16},{16,20},{20,24},{24,28},{1,5},{5,9},{9,... | collective-permute-start | bytes 393224 | tf_op jit(solution)/shard_map/while/body/eval_jaxpr/ppermute | solution.py:16
  76.8 4.3 %collective-permute-start = (bf16[256,2,128]{2,0,1:T(8,128)(2,1)}, bf16[256,2,128]{2,0,1:T(8,128)(2,1)S(1)}, u32[]{:S(2)}, u32[]{:S(2)}) collective-permute-start(bf16[256,2,128]{2,0,1:T(8,128)(2,1)} %get-tuple-element.308), channel_id=1, source_target_pairs={{0,4},{4,8},{8,12},{12,16},{16,20},{20,24},{24,28},{1,5},{5,9},{9,... | collective-permute-start | bytes 393224 | tf_op jit(solution)/shard_map/while/body/eval_jaxpr/ppermute | solution.py:16
  81.1 3.7 %collective-permute-start.1 = (bf16[256,2,128]{2,0,1:T(8,128)(2,1)S(1)}, bf16[256,2,128]{2,0,1:T(8,128)(2,1)S(1)}, u32[]{:S(2)}, u32[]{:S(2)}) collective-permute-start(bf16[256,2,128]{2,0,1:T(8,128)(2,1)S(1)} %get-tuple-element.309), channel_id=1, source_target_pairs={{0,4},{4,8},{8,12},{12,16},{16,20},{20,24},{24,28},{1,5},{5,9},{9,... | collective-permute-start | bytes 393224 | tf_op jit(solution)/shard_map/while/body/eval_jaxpr/ppermute | solution.py:16
  85.0 1.4 %fusion.40 = (f32[2,2,256]{2,1,0:T(2,128)S(1)}, bf16[2,2,256,256]{2,3,1,0:T(8,128)(2,1)S(1)}) fusion(bf16[256,2,2,128]{3,0,2,1:T(8,128)(2,1)} %get-tuple-element.323, bf16[256,2,128]{2,0,1:T(8,128)(2,1)S(1)} %collective-permute-done, pred[256,256]{0,1:T(8,128)(4,1)S(1)} %fusion.39), kind=kOutput, calls=%fused_computation.49.clone.1 | convolution fusion | flops 68418560 | bytes 987136 | tf_op jit(solution)/shard_map/while/body/eval_jaxpr/sgrh,kgh->grsk/dot_general | solution.py:41
  88.6 4.3 %collective-permute-start = (bf16[256,2,128]{2,0,1:T(8,128)(2,1)}, bf16[256,2,128]{2,0,1:T(8,128)(2,1)S(1)}, u32[]{:S(2)}, u32[]{:S(2)}) collective-permute-start(bf16[256,2,128]{2,0,1:T(8,128)(2,1)} %get-tuple-element.308), channel_id=1, source_target_pairs={{0,4},{4,8},{8,12},{12,16},{16,20},{20,24},{24,28},{1,5},{5,9},{9,... | collective-permute-start | bytes 393224 | tf_op jit(solution)/shard_map/while/body/eval_jaxpr/ppermute | solution.py:16
  92.9 4.6 %collective-permute-start.1 = (bf16[256,2,128]{2,0,1:T(8,128)(2,1)S(1)}, bf16[256,2,128]{2,0,1:T(8,128)(2,1)S(1)}, u32[]{:S(2)}, u32[]{:S(2)}) collective-permute-start(bf16[256,2,128]{2,0,1:T(8,128)(2,1)S(1)} %get-tuple-element.309), channel_id=1, source_target_pairs={{0,4},{4,8},{8,12},{12,16},{16,20},{20,24},{24,28},{1,5},{5,9},{9,... | collective-permute-start | bytes 393224 | tf_op jit(solution)/shard_map/while/body/eval_jaxpr/ppermute | solution.py:16
  97.7 1.4 %fusion.40 = (f32[2,2,256]{2,1,0:T(2,128)S(1)}, bf16[2,2,256,256]{2,3,1,0:T(8,128)(2,1)S(1)}) fusion(bf16[256,2,2,128]{3,0,2,1:T(8,128)(2,1)} %get-tuple-element.323, bf16[256,2,128]{2,0,1:T(8,128)(2,1)S(1)} %collective-permute-done, pred[256,256]{0,1:T(8,128)(4,1)S(1)} %fusion.39), kind=kOutput, calls=%fused_computation.49.clone.1 | convolution fusion | flops 68418560 | bytes 987136 | tf_op jit(solution)/shard_map/while/body/eval_jaxpr/sgrh,kgh->grsk/dot_general | solution.py:41
  101.2 2.0 %divide_convert_fusion = bf16[2,2,256,128]{3,2,1,0:T(8,128)(2,1)} fusion(f32[2,2,256,128]{3,2,1,0:T(8,128)} %get-tuple-element.189, f32[2,2,256]{2,1,0:T(2,128)S(1)} %get-tuple-element.190), kind=kLoop, calls=%fused_computation.26 | loop fusion | flops 262144 | bytes 790528 | tf_op jit(solution)/shard_map/convert_element_type | solution.py:97
  103.9 15.4 %all-gather.2.cloned.1.call-done = bf16[256,16,128]{2,0,1:T(8,128)(2,1)} async-done(((bf16[256,4,128]{2,0,1:T(8,128)(2,1)}), bf16[256,16,128]{2,0,1:T(8,128)(2,1)}) %all-gather.2.cloned.1.call-update) | async-done | bytes 1048592 | tf_op jit(solution)/shard_map/all_gather | solution.py:100
  119.3 3.1 %multiply_reduce_fusion = (f32[256]{0:T(256)S(1)}, f32[256,768]{1,0:T(8,128)}) fusion(bf16[256,16,128]{2,0,1:T(8,128)(2,1)} %all-gather.2.cloned.1.call-done, bf16[16,128,768]{2,1,0:T(8,128)(2,1)S(1)} %copy-done), kind=kOutput, calls=%fused_computation.25 | convolution fusion | flops 805699328 | bytes 4981760 | tf_op jit(solution)/shard_map/dot_general | solution.py:103
  122.4 5.9 %psum.7 = f32[256]{0:T(256)S(1)} all-reduce(f32[256]{0:T(256)S(1)} %get-tuple-element.233), channel_id=1, replica_groups=mesh['ctx'=8,'tp'=4] {'tp'}, use_global_device_ids=true, to_apply=%region_5.6 | all-reduce | flops 256 | bytes 2048 | tf_op jit(solution)/shard_map/psum | solution.py:106
  128.3 2.1 %add_convert_fusion = bf16[256,768]{1,0:T(8,128)(2,1)} fusion(f32[256,768]{1,0:T(8,128)} %get-tuple-element.234, bf16[256,768]{1,0:T(8,128)(2,1)S(1)} %copy-done.4, f32[768]{0:T(1024)S(1)} %convert_element_type.50, f32[256]{0:T(256)S(1)} %add_rsqrt_fusion), kind=kLoop, calls=%fused_computation.24 | loop fusion | flops 983040 | bytes 1576960 | tf_op jit(solution)/shard_map/convert_element_type | solution.py:109
  (133 shorter events, 30.1 us)
Async XLA Ops:
  6.5 112.8 %copy-start = (bf16[16,128,768]{2,1,0:T(8,128)(2,1)S(1)}, bf16[16,128,768]{2,1,0:T(8,128)(2,1)}, u32[]{:S(2)}) copy-start(bf16[16,128,768]{2,1,0:T(8,128)(2,1)} %param.12) | copy-start | bytes 9437188
  6.5 4.8 %copy-start.3 = (bf16[256,2,128]{2,1,0:T(2,128)(2,1)S(1)}, bf16[256,2,128]{2,1,0:T(2,128)(2,1)}, u32[]{:S(2)}) copy-start(bf16[256,2,128]{2,1,0:T(2,128)(2,1)} %param.10) | copy-start | bytes 393220
  6.5 112.8 %all-gather.2.cloned.1.call-start = ((), (), s32[]{:S(2)}) async-start(), calls=%async_computation | async-start | bytes 1310720 | tf_op jit(solution)/shard_map/all_gather | solution.py:100
  13.1 3.0 %copy-start.6 = (bf16[256,2,128]{2,0,1:T(8,128)(2,1)}, bf16[256,2,128]{2,0,1:T(8,128)(2,1)S(1)}, u32[]{:S(2)}) copy-start(bf16[256,2,128]{2,0,1:T(8,128)(2,1)S(1)} %pad_maximum_fusion.1) | copy-start | bytes 393220
  16.1 8.5 %collective-permute-start = (bf16[256,2,128]{2,0,1:T(8,128)(2,1)}, bf16[256,2,128]{2,0,1:T(8,128)(2,1)S(1)}, u32[]{:S(2)}, u32[]{:S(2)}) collective-permute-start(bf16[256,2,128]{2,0,1:T(8,128)(2,1)} %get-tuple-element.308), channel_id=1, source_target_pairs={{0,4},{4,8},{8,12},{12,16},{16,20},{20,24},{24,28},{1,5},{5,9},{9,... | collective-permute-start | bytes 393224 | tf_op jit(solution)/shard_map/while/body/eval_jaxpr/ppermute | solution.py:16
  21.0 5.9 %collective-permute-start.1 = (bf16[256,2,128]{2,0,1:T(8,128)(2,1)S(1)}, bf16[256,2,128]{2,0,1:T(8,128)(2,1)S(1)}, u32[]{:S(2)}, u32[]{:S(2)}) collective-permute-start(bf16[256,2,128]{2,0,1:T(8,128)(2,1)S(1)} %get-tuple-element.309), channel_id=1, source_target_pairs={{0,4},{4,8},{8,12},{12,16},{16,20},{20,24},{24,28},{1,5},{5,9},{9,... | collective-permute-start | bytes 393224 | tf_op jit(solution)/shard_map/while/body/eval_jaxpr/ppermute | solution.py:16
  24.5 2.5 %copy-start.1 = (f32[2,2,256,128]{3,2,1,0:T(8,128)S(1)}, f32[2,2,256,128]{3,2,1,0:T(8,128)}, u32[]{:S(2)}) copy-start(f32[2,2,256,128]{3,2,1,0:T(8,128)} %get-tuple-element.306) | copy-start | bytes 1572868 | tf_op jit(solution)/shard_map/while
  28.2 8.9 %collective-permute-start = (bf16[256,2,128]{2,0,1:T(8,128)(2,1)}, bf16[256,2,128]{2,0,1:T(8,128)(2,1)S(1)}, u32[]{:S(2)}, u32[]{:S(2)}) collective-permute-start(bf16[256,2,128]{2,0,1:T(8,128)(2,1)} %get-tuple-element.308), channel_id=1, source_target_pairs={{0,4},{4,8},{8,12},{12,16},{16,20},{20,24},{24,28},{1,5},{5,9},{9,... | collective-permute-start | bytes 393224 | tf_op jit(solution)/shard_map/while/body/eval_jaxpr/ppermute | solution.py:16
  32.5 6.8 %collective-permute-start.1 = (bf16[256,2,128]{2,0,1:T(8,128)(2,1)S(1)}, bf16[256,2,128]{2,0,1:T(8,128)(2,1)S(1)}, u32[]{:S(2)}, u32[]{:S(2)}) collective-permute-start(bf16[256,2,128]{2,0,1:T(8,128)(2,1)S(1)} %get-tuple-element.309), channel_id=1, source_target_pairs={{0,4},{4,8},{8,12},{12,16},{16,20},{20,24},{24,28},{1,5},{5,9},{9,... | collective-permute-start | bytes 393224 | tf_op jit(solution)/shard_map/while/body/eval_jaxpr/ppermute | solution.py:16
  36.9 2.5 %copy-start.1 = (f32[2,2,256,128]{3,2,1,0:T(8,128)S(1)}, f32[2,2,256,128]{3,2,1,0:T(8,128)}, u32[]{:S(2)}) copy-start(f32[2,2,256,128]{3,2,1,0:T(8,128)} %get-tuple-element.306) | copy-start | bytes 1572868 | tf_op jit(solution)/shard_map/while
  40.6 8.7 %collective-permute-start = (bf16[256,2,128]{2,0,1:T(8,128)(2,1)}, bf16[256,2,128]{2,0,1:T(8,128)(2,1)S(1)}, u32[]{:S(2)}, u32[]{:S(2)}) collective-permute-start(bf16[256,2,128]{2,0,1:T(8,128)(2,1)} %get-tuple-element.308), channel_id=1, source_target_pairs={{0,4},{4,8},{8,12},{12,16},{16,20},{20,24},{24,28},{1,5},{5,9},{9,... | collective-permute-start | bytes 393224 | tf_op jit(solution)/shard_map/while/body/eval_jaxpr/ppermute | solution.py:16
  45.0 6.6 %collective-permute-start.1 = (bf16[256,2,128]{2,0,1:T(8,128)(2,1)S(1)}, bf16[256,2,128]{2,0,1:T(8,128)(2,1)S(1)}, u32[]{:S(2)}, u32[]{:S(2)}) collective-permute-start(bf16[256,2,128]{2,0,1:T(8,128)(2,1)S(1)} %get-tuple-element.309), channel_id=1, source_target_pairs={{0,4},{4,8},{8,12},{12,16},{16,20},{20,24},{24,28},{1,5},{5,9},{9,... | collective-permute-start | bytes 393224 | tf_op jit(solution)/shard_map/while/body/eval_jaxpr/ppermute | solution.py:16
  49.1 2.5 %copy-start.1 = (f32[2,2,256,128]{3,2,1,0:T(8,128)S(1)}, f32[2,2,256,128]{3,2,1,0:T(8,128)}, u32[]{:S(2)}) copy-start(f32[2,2,256,128]{3,2,1,0:T(8,128)} %get-tuple-element.306) | copy-start | bytes 1572868 | tf_op jit(solution)/shard_map/while
  52.8 8.2 %collective-permute-start = (bf16[256,2,128]{2,0,1:T(8,128)(2,1)}, bf16[256,2,128]{2,0,1:T(8,128)(2,1)S(1)}, u32[]{:S(2)}, u32[]{:S(2)}) collective-permute-start(bf16[256,2,128]{2,0,1:T(8,128)(2,1)} %get-tuple-element.308), channel_id=1, source_target_pairs={{0,4},{4,8},{8,12},{12,16},{16,20},{20,24},{24,28},{1,5},{5,9},{9,... | collective-permute-start | bytes 393224 | tf_op jit(solution)/shard_map/while/body/eval_jaxpr/ppermute | solution.py:16
  57.2 6.2 %collective-permute-start.1 = (bf16[256,2,128]{2,0,1:T(8,128)(2,1)S(1)}, bf16[256,2,128]{2,0,1:T(8,128)(2,1)S(1)}, u32[]{:S(2)}, u32[]{:S(2)}) collective-permute-start(bf16[256,2,128]{2,0,1:T(8,128)(2,1)S(1)} %get-tuple-element.309), channel_id=1, source_target_pairs={{0,4},{4,8},{8,12},{12,16},{16,20},{20,24},{24,28},{1,5},{5,9},{9,... | collective-permute-start | bytes 393224 | tf_op jit(solution)/shard_map/while/body/eval_jaxpr/ppermute | solution.py:16
  60.9 2.5 %copy-start.1 = (f32[2,2,256,128]{3,2,1,0:T(8,128)S(1)}, f32[2,2,256,128]{3,2,1,0:T(8,128)}, u32[]{:S(2)}) copy-start(f32[2,2,256,128]{3,2,1,0:T(8,128)} %get-tuple-element.306) | copy-start | bytes 1572868 | tf_op jit(solution)/shard_map/while
  64.6 8.6 %collective-permute-start = (bf16[256,2,128]{2,0,1:T(8,128)(2,1)}, bf16[256,2,128]{2,0,1:T(8,128)(2,1)S(1)}, u32[]{:S(2)}, u32[]{:S(2)}) collective-permute-start(bf16[256,2,128]{2,0,1:T(8,128)(2,1)} %get-tuple-element.308), channel_id=1, source_target_pairs={{0,4},{4,8},{8,12},{12,16},{16,20},{20,24},{24,28},{1,5},{5,9},{9,... | collective-permute-start | bytes 393224 | tf_op jit(solution)/shard_map/while/body/eval_jaxpr/ppermute | solution.py:16
  69.0 6.6 %collective-permute-start.1 = (bf16[256,2,128]{2,0,1:T(8,128)(2,1)S(1)}, bf16[256,2,128]{2,0,1:T(8,128)(2,1)S(1)}, u32[]{:S(2)}, u32[]{:S(2)}) collective-permute-start(bf16[256,2,128]{2,0,1:T(8,128)(2,1)S(1)} %get-tuple-element.309), channel_id=1, source_target_pairs={{0,4},{4,8},{8,12},{12,16},{16,20},{20,24},{24,28},{1,5},{5,9},{9,... | collective-permute-start | bytes 393224 | tf_op jit(solution)/shard_map/while/body/eval_jaxpr/ppermute | solution.py:16
  73.1 2.5 %copy-start.1 = (f32[2,2,256,128]{3,2,1,0:T(8,128)S(1)}, f32[2,2,256,128]{3,2,1,0:T(8,128)}, u32[]{:S(2)}) copy-start(f32[2,2,256,128]{3,2,1,0:T(8,128)} %get-tuple-element.306) | copy-start | bytes 1572868 | tf_op jit(solution)/shard_map/while
  76.8 8.2 %collective-permute-start = (bf16[256,2,128]{2,0,1:T(8,128)(2,1)}, bf16[256,2,128]{2,0,1:T(8,128)(2,1)S(1)}, u32[]{:S(2)}, u32[]{:S(2)}) collective-permute-start(bf16[256,2,128]{2,0,1:T(8,128)(2,1)} %get-tuple-element.308), channel_id=1, source_target_pairs={{0,4},{4,8},{8,12},{12,16},{16,20},{20,24},{24,28},{1,5},{5,9},{9,... | collective-permute-start | bytes 393224 | tf_op jit(solution)/shard_map/while/body/eval_jaxpr/ppermute | solution.py:16
  81.1 6.2 %collective-permute-start.1 = (bf16[256,2,128]{2,0,1:T(8,128)(2,1)S(1)}, bf16[256,2,128]{2,0,1:T(8,128)(2,1)S(1)}, u32[]{:S(2)}, u32[]{:S(2)}) collective-permute-start(bf16[256,2,128]{2,0,1:T(8,128)(2,1)S(1)} %get-tuple-element.309), channel_id=1, source_target_pairs={{0,4},{4,8},{8,12},{12,16},{16,20},{20,24},{24,28},{1,5},{5,9},{9,... | collective-permute-start | bytes 393224 | tf_op jit(solution)/shard_map/while/body/eval_jaxpr/ppermute | solution.py:16
  88.6 9.1 %collective-permute-start = (bf16[256,2,128]{2,0,1:T(8,128)(2,1)}, bf16[256,2,128]{2,0,1:T(8,128)(2,1)S(1)}, u32[]{:S(2)}, u32[]{:S(2)}) collective-permute-start(bf16[256,2,128]{2,0,1:T(8,128)(2,1)} %get-tuple-element.308), channel_id=1, source_target_pairs={{0,4},{4,8},{8,12},{12,16},{16,20},{20,24},{24,28},{1,5},{5,9},{9,... | collective-permute-start | bytes 393224 | tf_op jit(solution)/shard_map/while/body/eval_jaxpr/ppermute | solution.py:16
  92.9 7.1 %collective-permute-start.1 = (bf16[256,2,128]{2,0,1:T(8,128)(2,1)S(1)}, bf16[256,2,128]{2,0,1:T(8,128)(2,1)S(1)}, u32[]{:S(2)}, u32[]{:S(2)}) collective-permute-start(bf16[256,2,128]{2,0,1:T(8,128)(2,1)S(1)} %get-tuple-element.309), channel_id=1, source_target_pairs={{0,4},{4,8},{8,12},{12,16},{16,20},{20,24},{24,28},{1,5},{5,9},{9,... | collective-permute-start | bytes 393224 | tf_op jit(solution)/shard_map/while/body/eval_jaxpr/ppermute | solution.py:16
  101.2 27.1 %copy-start.4 = (bf16[256,768]{1,0:T(8,128)(2,1)S(1)}, bf16[256,768]{1,0:T(8,128)(2,1)}, u32[]{:S(2)}) copy-start(bf16[256,768]{1,0:T(8,128)(2,1)} %param.11) | copy-start | bytes 1179652
  (11 other events, 14.2 us)
Sparse Core Ops, SparseCore 0:
  103.4 15.8 all-gather.1
where the time goes:
time: 138 us; the launch traced here: 137 us
  starting transfers between devices  58.8 us (43%)
  matrix products  17.8 us (13%)
  waiting for transfers between devices  16.7 us (12%)
  between operations  13.5 us (10%)
  other arithmetic  12.3 us (9%)
  local copies, waits for them, and re-layouts  11.6 us (8%)
  blocking collectives  5.85 us (4%)
    ppermute x14, starting transfers between devices, passed_along(): lax.ppermute(value, axis, [(source, source + steps) for source in range(f...  58.8 us
    all_gather x1, waiting for transfers between devices, local(): piece = lax.all_gather(attended, 'tp', axis=1, tiled=True)  15.4 us
    dot_general x8, matrix products, attend_block(): jnp.einsum('sgrh,kgh->grsk', rotary_queries, key_block, preferred_element...  10.6 us
    while x42, local copies, waits for them, and re-layouts  10.1 us
    psum x1, blocking collectives, local(): square_sums = lax.psum(jnp.sum(projected * projected, axis=1), 'tp')  5.85 us
    dot_general x8, matrix products, attend_block(): jnp.einsum('grsk,kgh->grsh', weights.astype(jnp.bfloat16), value_block, p...  4.09 us
    dot_general x1, matrix products, local(): jnp.dot(piece.reshape(rows, heads_in * head_size), weight_rows, preferred...  3.14 us
  transfers between devices with their start and end apart: 15, of which 8 were waited for; matrix products, arithmetic and copies ran while one was open for 12% of the time, Pallas kernels for 0%

commit v1 on v0

--- a/solution.py
+++ b/solution.py
@@ -8,6 +8,12 @@
 softcap_value = 50.0
 query_scale = 1.0 / 12.0
 rope_base = 10000.0
+
+
+def gather_and_add(x, name):
+    shards = lax.all_gather(x, name, axis=0, tiled=False)
+    total = shards.sum(axis=0)
+    return total
 
 
 def passed_along(value, axis, steps):
@@ -103,7 +109,7 @@
     projected = jnp.dot(
         piece.reshape(rows, heads_in * head_size), weight_rows, preferred_element_type=jnp.float32
     )
-    square_sums = lax.psum(jnp.sum(projected * projected, axis=1), "tp")
+    square_sums = gather_and_add(jnp.sum(projected * projected, axis=1), "tp")
     normed = projected * lax.rsqrt(square_sums / D + 1e-06)[:, None] * post_gain.astype(jnp.float32)
     mixed = residual.astype(jnp.float32) + normed
     return mixed.astype(jnp.bfloat16)

time: 138 us -> 137 us (level)
    psum x1 -> x0, blocking collectives: 5.85 us -> none  [local(): square_sums = lax.psum(jnp.sum(projected * projected, axis=1), 'tp')]
    all_gather x0 -> x1, blocking collectives: none -> 5.06 us  [gather_and_add(): shards = lax.all_gather(x, name, axis=0, tiled=False)]
where the time goes in v1:
time: 137 us; the launch traced here: 136 us
  starting transfers between devices  58.8 us (43%)
  matrix products  17.8 us (13%)
  waiting for transfers between devices  16.7 us (12%)
  between operations  13.5 us (10%)
  other arithmetic  12.3 us (9%)
  local copies, waits for them, and re-layouts  11.6 us (8%)
  blocking collectives  5.06 us (4%)
    ppermute x14, starting transfers between devices, passed_along(): lax.ppermute(value, axis, [(source, source + steps) for source in range(f...  58.8 us
    all_gather x1, waiting for transfers between devices, local(): piece = lax.all_gather(attended, 'tp', axis=1, tiled=True)  15.4 us
    dot_general x8, matrix products, attend_block(): jnp.einsum('sgrh,kgh->grsk', rotary_queries, key_block, preferred_element...  10.6 us
    while x42, local copies, waits for them, and re-layouts  10.1 us
    all_gather x1, blocking collectives, gather_and_add(): shards = lax.all_gather(x, name, axis=0, tiled=False)  5.06 us
    dot_general x8, matrix products, attend_block(): jnp.einsum('grsk,kgh->grsh', weights.astype(jnp.bfloat16), value_block, p...  4.09 us
    dot_general x1, matrix products, local(): jnp.dot(piece.reshape(rows, heads_in * head_size), weight_rows, preferred...  3.14 us
  transfers between devices with their start and end apart: 15, of which 8 were waited for; matrix products, arithmetic and copies ran while one was open for 12% of the time, Pallas kernels for 0%

profile of v1, /device:TPU:0, one launch (start us, length us, event | category | flops | bytes accessed | tf_op | source)
XLA Modules:
  0.0 136.5 jit_solution(18267356902781982223)
XLA Ops:
  16.1 85.1 %while.21 = (s32[]{:T(128)}, f32[2,2,256,128]{3,2,1,0:T(8,128)}, f32[2,2,256]{2,1,0:T(2,128)S(1)}, bf16[256,2,128]{2,0,1:T(8,128)(2,1)}, bf16[256,2,128]{2,0,1:T...) while((s32[]{:T(128)}, f32[2,2,256,128]{3,2,1,0:T(8,128)}, ...), condition=%wide.region_3.4_spmd, body=%wide.region_1.3_spmd.sunk | while | flops 135988224 | bytes 8540965 | solution.py:99
  16.1 4.9 %collective-permute-start = (bf16[256,2,128]{2,0,1:T(8,128)(2,1)}, bf16[256,2,128]{2,0,1:T(8,128)(2,1)S(1)}, u32[]{:S(2)}, u32[]{:S(2)}) collective-permute-start(bf16[256,2,128]{2,0,1:T(8,128)(2,1)} %get-tuple-element.308), channel_id=1, source_target_pairs={{0,4},{4,8},{8,12},{12,16},{16,20},{20,24},{24,28},{1,5},{5,9},{9,... | collective-permute-start | bytes 393224 | tf_op jit(solution)/shard_map/while/body/eval_jaxpr/ppermute | solution.py:22
  21.0 3.4 %collective-permute-start.1 = (bf16[256,2,128]{2,0,1:T(8,128)(2,1)S(1)}, bf16[256,2,128]{2,0,1:T(8,128)(2,1)S(1)}, u32[]{:S(2)}, u32[]{:S(2)}) collective-permute-start(bf16[256,2,128]{2,0,1:T(8,128)(2,1)S(1)} %get-tuple-element.309), channel_id=1, source_target_pairs={{0,4},{4,8},{8,12},{12,16},{16,20},{20,24},{24,28},{1,5},{5,9},{9,... | collective-permute-start | bytes 393224 | tf_op jit(solution)/shard_map/while/body/eval_jaxpr/ppermute | solution.py:22
  24.7 1.4 %fusion.40 = (f32[2,2,256]{2,1,0:T(2,128)S(1)}, bf16[2,2,256,256]{2,3,1,0:T(8,128)(2,1)S(1)}) fusion(bf16[256,2,2,128]{3,0,2,1:T(8,128)(2,1)} %get-tuple-element.323, bf16[256,2,128]{2,0,1:T(8,128)(2,1)S(1)} %collective-permute-done, pred[256,256]{0,1:T(8,128)(4,1)S(1)} %fusion.39), kind=kOutput, calls=%fused_computation.49.clone.1 | convolution fusion | flops 68418560 | bytes 987136 | tf_op jit(solution)/shard_map/while/body/eval_jaxpr/sgrh,kgh->grsk/dot_general | solution.py:47
  28.2 4.3 %collective-permute-start = (bf16[256,2,128]{2,0,1:T(8,128)(2,1)}, bf16[256,2,128]{2,0,1:T(8,128)(2,1)S(1)}, u32[]{:S(2)}, u32[]{:S(2)}) collective-permute-start(bf16[256,2,128]{2,0,1:T(8,128)(2,1)} %get-tuple-element.308), channel_id=1, source_target_pairs={{0,4},{4,8},{8,12},{12,16},{16,20},{20,24},{24,28},{1,5},{5,9},{9,... | collective-permute-start | bytes 393224 | tf_op jit(solution)/shard_map/while/body/eval_jaxpr/ppermute | solution.py:22
  32.5 4.3 %collective-permute-start.1 = (bf16[256,2,128]{2,0,1:T(8,128)(2,1)S(1)}, bf16[256,2,128]{2,0,1:T(8,128)(2,1)S(1)}, u32[]{:S(2)}, u32[]{:S(2)}) collective-permute-start(bf16[256,2,128]{2,0,1:T(8,128)(2,1)S(1)} %get-tuple-element.309), channel_id=1, source_target_pairs={{0,4},{4,8},{8,12},{12,16},{16,20},{20,24},{24,28},{1,5},{5,9},{9,... | collective-permute-start | bytes 393224 | tf_op jit(solution)/shard_map/while/body/eval_jaxpr/ppermute | solution.py:22
  40.6 4.3 %collective-permute-start = (bf16[256,2,128]{2,0,1:T(8,128)(2,1)}, bf16[256,2,128]{2,0,1:T(8,128)(2,1)S(1)}, u32[]{:S(2)}, u32[]{:S(2)}) collective-permute-start(bf16[256,2,128]{2,0,1:T(8,128)(2,1)} %get-tuple-element.308), channel_id=1, source_target_pairs={{0,4},{4,8},{8,12},{12,16},{16,20},{20,24},{24,28},{1,5},{5,9},{9,... | collective-permute-start | bytes 393224 | tf_op jit(solution)/shard_map/while/body/eval_jaxpr/ppermute | solution.py:22
  45.0 4.1 %collective-permute-start.1 = (bf16[256,2,128]{2,0,1:T(8,128)(2,1)S(1)}, bf16[256,2,128]{2,0,1:T(8,128)(2,1)S(1)}, u32[]{:S(2)}, u32[]{:S(2)}) collective-permute-start(bf16[256,2,128]{2,0,1:T(8,128)(2,1)S(1)} %get-tuple-element.309), channel_id=1, source_target_pairs={{0,4},{4,8},{8,12},{12,16},{16,20},{20,24},{24,28},{1,5},{5,9},{9,... | collective-permute-start | bytes 393224 | tf_op jit(solution)/shard_map/while/body/eval_jaxpr/ppermute | solution.py:22
  52.8 4.4 %collective-permute-start = (bf16[256,2,128]{2,0,1:T(8,128)(2,1)}, bf16[256,2,128]{2,0,1:T(8,128)(2,1)S(1)}, u32[]{:S(2)}, u32[]{:S(2)}) collective-permute-start(bf16[256,2,128]{2,0,1:T(8,128)(2,1)} %get-tuple-element.308), channel_id=1, source_target_pairs={{0,4},{4,8},{8,12},{12,16},{16,20},{20,24},{24,28},{1,5},{5,9},{9,... | collective-permute-start | bytes 393224 | tf_op jit(solution)/shard_map/while/body/eval_jaxpr/ppermute | solution.py:22
  57.2 3.7 %collective-permute-start.1 = (bf16[256,2,128]{2,0,1:T(8,128)(2,1)S(1)}, bf16[256,2,128]{2,0,1:T(8,128)(2,1)S(1)}, u32[]{:S(2)}, u32[]{:S(2)}) collective-permute-start(bf16[256,2,128]{2,0,1:T(8,128)(2,1)S(1)} %get-tuple-element.309), channel_id=1, source_target_pairs={{0,4},{4,8},{8,12},{12,16},{16,20},{20,24},{24,28},{1,5},{5,9},{9,... | collective-permute-start | bytes 393224 | tf_op jit(solution)/shard_map/while/body/eval_jaxpr/ppermute | solution.py:22
  61.1 1.4 %fusion.40 = (f32[2,2,256]{2,1,0:T(2,128)S(1)}, bf16[2,2,256,256]{2,3,1,0:T(8,128)(2,1)S(1)}) fusion(bf16[256,2,2,128]{3,0,2,1:T(8,128)(2,1)} %get-tuple-element.323, bf16[256,2,128]{2,0,1:T(8,128)(2,1)S(1)} %collective-permute-done, pred[256,256]{0,1:T(8,128)(4,1)S(1)} %fusion.39), kind=kOutput, calls=%fused_computation.49.clone.1 | convolution fusion | flops 68418560 | bytes 987136 | tf_op jit(solution)/shard_map/while/body/eval_jaxpr/sgrh,kgh->grsk/dot_general | solution.py:47
  64.6 4.3 %collective-permute-start = (bf16[256,2,128]{2,0,1:T(8,128)(2,1)}, bf16[256,2,128]{2,0,1:T(8,128)(2,1)S(1)}, u32[]{:S(2)}, u32[]{:S(2)}) collective-permute-start(bf16[256,2,128]{2,0,1:T(8,128)(2,1)} %get-tuple-element.308), channel_id=1, source_target_pairs={{0,4},{4,8},{8,12},{12,16},{16,20},{20,24},{24,28},{1,5},{5,9},{9,... | collective-permute-start | bytes 393224 | tf_op jit(solution)/shard_map/while/body/eval_jaxpr/ppermute | solution.py:22
  69.0 4.1 %collective-permute-start.1 = (bf16[256,2,128]{2,0,1:T(8,128)(2,1)S(1)}, bf16[256,2,128]{2,0,1:T(8,128)(2,1)S(1)}, u32[]{:S(2)}, u32[]{:S(2)}) collective-permute-start(bf16[256,2,128]{2,0,1:T(8,128)(2,1)S(1)} %get-tuple-element.309), channel_id=1, source_target_pairs={{0,4},{4,8},{8,12},{12,16},{16,20},{20,24},{24,28},{1,5},{5,9},{9,... | collective-permute-start | bytes 393224 | tf_op jit(solution)/shard_map/while/body/eval_jaxpr/ppermute | solution.py:22
  76.8 4.3 %collective-permute-start = (bf16[256,2,128]{2,0,1:T(8,128)(2,1)}, bf16[256,2,128]{2,0,1:T(8,128)(2,1)S(1)}, u32[]{:S(2)}, u32[]{:S(2)}) collective-permute-start(bf16[256,2,128]{2,0,1:T(8,128)(2,1)} %get-tuple-element.308), channel_id=1, source_target_pairs={{0,4},{4,8},{8,12},{12,16},{16,20},{20,24},{24,28},{1,5},{5,9},{9,... | collective-permute-start | bytes 393224 | tf_op jit(solution)/shard_map/while/body/eval_jaxpr/ppermute | solution.py:22
  81.1 3.7 %collective-permute-start.1 = (bf16[256,2,128]{2,0,1:T(8,128)(2,1)S(1)}, bf16[256,2,128]{2,0,1:T(8,128)(2,1)S(1)}, u32[]{:S(2)}, u32[]{:S(2)}) collective-permute-start(bf16[256,2,128]{2,0,1:T(8,128)(2,1)S(1)} %get-tuple-element.309), channel_id=1, source_target_pairs={{0,4},{4,8},{8,12},{12,16},{16,20},{20,24},{24,28},{1,5},{5,9},{9,... | collective-permute-start | bytes 393224 | tf_op jit(solution)/shard_map/while/body/eval_jaxpr/ppermute | solution.py:22
  85.0 1.4 %fusion.40 = (f32[2,2,256]{2,1,0:T(2,128)S(1)}, bf16[2,2,256,256]{2,3,1,0:T(8,128)(2,1)S(1)}) fusion(bf16[256,2,2,128]{3,0,2,1:T(8,128)(2,1)} %get-tuple-element.323, bf16[256,2,128]{2,0,1:T(8,128)(2,1)S(1)} %collective-permute-done, pred[256,256]{0,1:T(8,128)(4,1)S(1)} %fusion.39), kind=kOutput, calls=%fused_computation.49.clone.1 | convolution fusion | flops 68418560 | bytes 987136 | tf_op jit(solution)/shard_map/while/body/eval_jaxpr/sgrh,kgh->grsk/dot_general | solution.py:47
  88.6 4.3 %collective-permute-start = (bf16[256,2,128]{2,0,1:T(8,128)(2,1)}, bf16[256,2,128]{2,0,1:T(8,128)(2,1)S(1)}, u32[]{:S(2)}, u32[]{:S(2)}) collective-permute-start(bf16[256,2,128]{2,0,1:T(8,128)(2,1)} %get-tuple-element.308), channel_id=1, source_target_pairs={{0,4},{4,8},{8,12},{12,16},{16,20},{20,24},{24,28},{1,5},{5,9},{9,... | collective-permute-start | bytes 393224 | tf_op jit(solution)/shard_map/while/body/eval_jaxpr/ppermute | solution.py:22
  92.9 4.6 %collective-permute-start.1 = (bf16[256,2,128]{2,0,1:T(8,128)(2,1)S(1)}, bf16[256,2,128]{2,0,1:T(8,128)(2,1)S(1)}, u32[]{:S(2)}, u32[]{:S(2)}) collective-permute-start(bf16[256,2,128]{2,0,1:T(8,128)(2,1)S(1)} %get-tuple-element.309), channel_id=1, source_target_pairs={{0,4},{4,8},{8,12},{12,16},{16,20},{20,24},{24,28},{1,5},{5,9},{9,... | collective-permute-start | bytes 393224 | tf_op jit(solution)/shard_map/while/body/eval_jaxpr/ppermute | solution.py:22
  97.7 1.4 %fusion.40 = (f32[2,2,256]{2,1,0:T(2,128)S(1)}, bf16[2,2,256,256]{2,3,1,0:T(8,128)(2,1)S(1)}) fusion(bf16[256,2,2,128]{3,0,2,1:T(8,128)(2,1)} %get-tuple-element.323, bf16[256,2,128]{2,0,1:T(8,128)(2,1)S(1)} %collective-permute-done, pred[256,256]{0,1:T(8,128)(4,1)S(1)} %fusion.39), kind=kOutput, calls=%fused_computation.49.clone.1 | convolution fusion | flops 68418560 | bytes 987136 | tf_op jit(solution)/shard_map/while/body/eval_jaxpr/sgrh,kgh->grsk/dot_general | solution.py:47
  101.2 2.0 %divide_convert_fusion = bf16[2,2,256,128]{3,2,1,0:T(8,128)(2,1)} fusion(f32[2,2,256,128]{3,2,1,0:T(8,128)} %get-tuple-element.189, f32[2,2,256]{2,1,0:T(2,128)S(1)} %get-tuple-element.190), kind=kLoop, calls=%fused_computation.26 | loop fusion | flops 262144 | bytes 790528 | tf_op jit(solution)/shard_map/convert_element_type | solution.py:103
  103.9 15.4 %all-gather.4.cloned.1.call-done = bf16[256,16,128]{2,0,1:T(8,128)(2,1)} async-done(((bf16[256,4,128]{2,0,1:T(8,128)(2,1)}), bf16[256,16,128]{2,0,1:T(8,128)(2,1)}) %all-gather.4.cloned.1.call-update) | async-done | bytes 1048592 | tf_op jit(solution)/shard_map/all_gather | solution.py:106
  119.3 3.1 %multiply_reduce_fusion = (f32[256]{0:T(256)S(1)}, f32[256,768]{1,0:T(8,128)}) fusion(bf16[256,16,128]{2,0,1:T(8,128)(2,1)} %all-gather.4.cloned.1.call-done, bf16[16,128,768]{2,1,0:T(8,128)(2,1)S(1)} %copy-done), kind=kOutput, calls=%fused_computation.25 | convolution fusion | flops 805699328 | bytes 4981760 | tf_op jit(solution)/shard_map/dot_general | solution.py:109
  122.4 5.1 %all-gather.1 = f32[4,1,256]{2,1,0:T(1,128)S(1)} all-gather(f32[1,1,256]{2,1,0:T(1,128)S(1)} %bitcast.54), channel_id=2, replica_groups=mesh['ctx'=8,'tp'=4] {'tp'}, dimensions={0}, use_global_device_ids=true | all-gather | bytes 5120 | tf_op jit(solution)/shard_map/all_gather | solution.py:14
  127.5 2.1 %add_convert_fusion = bf16[256,768]{1,0:T(8,128)(2,1)} fusion(f32[256,768]{1,0:T(8,128)} %get-tuple-element.234, bf16[256,768]{1,0:T(8,128)(2,1)S(1)} %copy-done.4, f32[768]{0:T(1024)S(1)} %convert_element_type.50, f32[256]{0:T(256)S(1)} %add_rsqrt_fusion), kind=kLoop, calls=%fused_computation.24 | loop fusion | flops 983040 | bytes 1576960 | tf_op jit(solution)/shard_map/convert_element_type | solution.py:115
  (134 shorter events, 30.1 us)
Async XLA Ops:
  6.5 112.8 %copy-start = (bf16[16,128,768]{2,1,0:T(8,128)(2,1)S(1)}, bf16[16,128,768]{2,1,0:T(8,128)(2,1)}, u32[]{:S(2)}) copy-start(bf16[16,128,768]{2,1,0:T(8,128)(2,1)} %param.12) | copy-start | bytes 9437188
  6.5 4.8 %copy-start.3 = (bf16[256,2,128]{2,1,0:T(2,128)(2,1)S(1)}, bf16[256,2,128]{2,1,0:T(2,128)(2,1)}, u32[]{:S(2)}) copy-start(bf16[256,2,128]{2,1,0:T(2,128)(2,1)} %param.10) | copy-start | bytes 393220
  6.5 112.8 %all-gather.4.cloned.1.call-start = ((), (), s32[]{:S(2)}) async-start(), calls=%async_computation | async-start | bytes 1310720 | tf_op jit(solution)/shard_map/all_gather | solution.py:106
  13.1 3.0 %copy-start.6 = (bf16[256,2,128]{2,0,1:T(8,128)(2,1)}, bf16[256,2,128]{2,0,1:T(8,128)(2,1)S(1)}, u32[]{:S(2)}) copy-start(bf16[256,2,128]{2,0,1:T(8,128)(2,1)S(1)} %pad_maximum_fusion.1) | copy-start | bytes 393220
  16.1 8.5 %collective-permute-start = (bf16[256,2,128]{2,0,1:T(8,128)(2,1)}, bf16[256,2,128]{2,0,1:T(8,128)(2,1)S(1)}, u32[]{:S(2)}, u32[]{:S(2)}) collective-permute-start(bf16[256,2,128]{2,0,1:T(8,128)(2,1)} %get-tuple-element.308), channel_id=1, source_target_pairs={{0,4},{4,8},{8,12},{12,16},{16,20},{20,24},{24,28},{1,5},{5,9},{9,... | collective-permute-start | bytes 393224 | tf_op jit(solution)/shard_map/while/body/eval_jaxpr/ppermute | solution.py:22
  21.0 5.9 %collective-permute-start.1 = (bf16[256,2,128]{2,0,1:T(8,128)(2,1)S(1)}, bf16[256,2,128]{2,0,1:T(8,128)(2,1)S(1)}, u32[]{:S(2)}, u32[]{:S(2)}) collective-permute-start(bf16[256,2,128]{2,0,1:T(8,128)(2,1)S(1)} %get-tuple-element.309), channel_id=1, source_target_pairs={{0,4},{4,8},{8,12},{12,16},{16,20},{20,24},{24,28},{1,5},{5,9},{9,... | collective-permute-start | bytes 393224 | tf_op jit(solution)/shard_map/while/body/eval_jaxpr/ppermute | solution.py:22
  24.5 2.5 %copy-start.1 = (f32[2,2,256,128]{3,2,1,0:T(8,128)S(1)}, f32[2,2,256,128]{3,2,1,0:T(8,128)}, u32[]{:S(2)}) copy-start(f32[2,2,256,128]{3,2,1,0:T(8,128)} %get-tuple-element.306) | copy-start | bytes 1572868 | tf_op jit(solution)/shard_map/while
  28.2 8.9 %collective-permute-start = (bf16[256,2,128]{2,0,1:T(8,128)(2,1)}, bf16[256,2,128]{2,0,1:T(8,128)(2,1)S(1)}, u32[]{:S(2)}, u32[]{:S(2)}) collective-permute-start(bf16[256,2,128]{2,0,1:T(8,128)(2,1)} %get-tuple-element.308), channel_id=1, source_target_pairs={{0,4},{4,8},{8,12},{12,16},{16,20},{20,24},{24,28},{1,5},{5,9},{9,... | collective-permute-start | bytes 393224 | tf_op jit(solution)/shard_map/while/body/eval_jaxpr/ppermute | solution.py:22
  32.5 6.8 %collective-permute-start.1 = (bf16[256,2,128]{2,0,1:T(8,128)(2,1)S(1)}, bf16[256,2,128]{2,0,1:T(8,128)(2,1)S(1)}, u32[]{:S(2)}, u32[]{:S(2)}) collective-permute-start(bf16[256,2,128]{2,0,1:T(8,128)(2,1)S(1)} %get-tuple-element.309), channel_id=1, source_target_pairs={{0,4},{4,8},{8,12},{12,16},{16,20},{20,24},{24,28},{1,5},{5,9},{9,... | collective-permute-start | bytes 393224 | tf_op jit(solution)/shard_map/while/body/eval_jaxpr/ppermute | solution.py:22
  36.9 2.5 %copy-start.1 = (f32[2,2,256,128]{3,2,1,0:T(8,128)S(1)}, f32[2,2,256,128]{3,2,1,0:T(8,128)}, u32[]{:S(2)}) copy-start(f32[2,2,256,128]{3,2,1,0:T(8,128)} %get-tuple-element.306) | copy-start | bytes 1572868 | tf_op jit(solution)/shard_map/while
  40.6 8.7 %collective-permute-start = (bf16[256,2,128]{2,0,1:T(8,128)(2,1)}, bf16[256,2,128]{2,0,1:T(8,128)(2,1)S(1)}, u32[]{:S(2)}, u32[]{:S(2)}) collective-permute-start(bf16[256,2,128]{2,0,1:T(8,128)(2,1)} %get-tuple-element.308), channel_id=1, source_target_pairs={{0,4},{4,8},{8,12},{12,16},{16,20},{20,24},{24,28},{1,5},{5,9},{9,... | collective-permute-start | bytes 393224 | tf_op jit(solution)/shard_map/while/body/eval_jaxpr/ppermute | solution.py:22
  45.0 6.6 %collective-permute-start.1 = (bf16[256,2,128]{2,0,1:T(8,128)(2,1)S(1)}, bf16[256,2,128]{2,0,1:T(8,128)(2,1)S(1)}, u32[]{:S(2)}, u32[]{:S(2)}) collective-permute-start(bf16[256,2,128]{2,0,1:T(8,128)(2,1)S(1)} %get-tuple-element.309), channel_id=1, source_target_pairs={{0,4},{4,8},{8,12},{12,16},{16,20},{20,24},{24,28},{1,5},{5,9},{9,... | collective-permute-start | bytes 393224 | tf_op jit(solution)/shard_map/while/body/eval_jaxpr/ppermute | solution.py:22
  49.1 2.5 %copy-start.1 = (f32[2,2,256,128]{3,2,1,0:T(8,128)S(1)}, f32[2,2,256,128]{3,2,1,0:T(8,128)}, u32[]{:S(2)}) copy-start(f32[2,2,256,128]{3,2,1,0:T(8,128)} %get-tuple-element.306) | copy-start | bytes 1572868 | tf_op jit(solution)/shard_map/while
  52.8 8.2 %collective-permute-start = (bf16[256,2,128]{2,0,1:T(8,128)(2,1)}, bf16[256,2,128]{2,0,1:T(8,128)(2,1)S(1)}, u32[]{:S(2)}, u32[]{:S(2)}) collective-permute-start(bf16[256,2,128]{2,0,1:T(8,128)(2,1)} %get-tuple-element.308), channel_id=1, source_target_pairs={{0,4},{4,8},{8,12},{12,16},{16,20},{20,24},{24,28},{1,5},{5,9},{9,... | collective-permute-start | bytes 393224 | tf_op jit(solution)/shard_map/while/body/eval_jaxpr/ppermute | solution.py:22
  57.2 6.2 %collective-permute-start.1 = (bf16[256,2,128]{2,0,1:T(8,128)(2,1)S(1)}, bf16[256,2,128]{2,0,1:T(8,128)(2,1)S(1)}, u32[]{:S(2)}, u32[]{:S(2)}) collective-permute-start(bf16[256,2,128]{2,0,1:T(8,128)(2,1)S(1)} %get-tuple-element.309), channel_id=1, source_target_pairs={{0,4},{4,8},{8,12},{12,16},{16,20},{20,24},{24,28},{1,5},{5,9},{9,... | collective-permute-start | bytes 393224 | tf_op jit(solution)/shard_map/while/body/eval_jaxpr/ppermute | solution.py:22
  60.9 2.5 %copy-start.1 = (f32[2,2,256,128]{3,2,1,0:T(8,128)S(1)}, f32[2,2,256,128]{3,2,1,0:T(8,128)}, u32[]{:S(2)}) copy-start(f32[2,2,256,128]{3,2,1,0:T(8,128)} %get-tuple-element.306) | copy-start | bytes 1572868 | tf_op jit(solution)/shard_map/while
  64.6 8.6 %collective-permute-start = (bf16[256,2,128]{2,0,1:T(8,128)(2,1)}, bf16[256,2,128]{2,0,1:T(8,128)(2,1)S(1)}, u32[]{:S(2)}, u32[]{:S(2)}) collective-permute-start(bf16[256,2,128]{2,0,1:T(8,128)(2,1)} %get-tuple-element.308), channel_id=1, source_target_pairs={{0,4},{4,8},{8,12},{12,16},{16,20},{20,24},{24,28},{1,5},{5,9},{9,... | collective-permute-start | bytes 393224 | tf_op jit(solution)/shard_map/while/body/eval_jaxpr/ppermute | solution.py:22
  69.0 6.6 %collective-permute-start.1 = (bf16[256,2,128]{2,0,1:T(8,128)(2,1)S(1)}, bf16[256,2,128]{2,0,1:T(8,128)(2,1)S(1)}, u32[]{:S(2)}, u32[]{:S(2)}) collective-permute-start(bf16[256,2,128]{2,0,1:T(8,128)(2,1)S(1)} %get-tuple-element.309), channel_id=1, source_target_pairs={{0,4},{4,8},{8,12},{12,16},{16,20},{20,24},{24,28},{1,5},{5,9},{9,... | collective-permute-start | bytes 393224 | tf_op jit(solution)/shard_map/while/body/eval_jaxpr/ppermute | solution.py:22
  73.1 2.5 %copy-start.1 = (f32[2,2,256,128]{3,2,1,0:T(8,128)S(1)}, f32[2,2,256,128]{3,2,1,0:T(8,128)}, u32[]{:S(2)}) copy-start(f32[2,2,256,128]{3,2,1,0:T(8,128)} %get-tuple-element.306) | copy-start | bytes 1572868 | tf_op jit(solution)/shard_map/while
  76.8 8.2 %collective-permute-start = (bf16[256,2,128]{2,0,1:T(8,128)(2,1)}, bf16[256,2,128]{2,0,1:T(8,128)(2,1)S(1)}, u32[]{:S(2)}, u32[]{:S(2)}) collective-permute-start(bf16[256,2,128]{2,0,1:T(8,128)(2,1)} %get-tuple-element.308), channel_id=1, source_target_pairs={{0,4},{4,8},{8,12},{12,16},{16,20},{20,24},{24,28},{1,5},{5,9},{9,... | collective-permute-start | bytes 393224 | tf_op jit(solution)/shard_map/while/body/eval_jaxpr/ppermute | solution.py:22
  81.1 6.2 %collective-permute-start.1 = (bf16[256,2,128]{2,0,1:T(8,128)(2,1)S(1)}, bf16[256,2,128]{2,0,1:T(8,128)(2,1)S(1)}, u32[]{:S(2)}, u32[]{:S(2)}) collective-permute-start(bf16[256,2,128]{2,0,1:T(8,128)(2,1)S(1)} %get-tuple-element.309), channel_id=1, source_target_pairs={{0,4},{4,8},{8,12},{12,16},{16,20},{20,24},{24,28},{1,5},{5,9},{9,... | collective-permute-start | bytes 393224 | tf_op jit(solution)/shard_map/while/body/eval_jaxpr/ppermute | solution.py:22
  88.6 9.1 %collective-permute-start = (bf16[256,2,128]{2,0,1:T(8,128)(2,1)}, bf16[256,2,128]{2,0,1:T(8,128)(2,1)S(1)}, u32[]{:S(2)}, u32[]{:S(2)}) collective-permute-start(bf16[256,2,128]{2,0,1:T(8,128)(2,1)} %get-tuple-element.308), channel_id=1, source_target_pairs={{0,4},{4,8},{8,12},{12,16},{16,20},{20,24},{24,28},{1,5},{5,9},{9,... | collective-permute-start | bytes 393224 | tf_op jit(solution)/shard_map/while/body/eval_jaxpr/ppermute | solution.py:22
  92.9 7.1 %collective-permute-start.1 = (bf16[256,2,128]{2,0,1:T(8,128)(2,1)S(1)}, bf16[256,2,128]{2,0,1:T(8,128)(2,1)S(1)}, u32[]{:S(2)}, u32[]{:S(2)}) collective-permute-start(bf16[256,2,128]{2,0,1:T(8,128)(2,1)S(1)} %get-tuple-element.309), channel_id=1, source_target_pairs={{0,4},{4,8},{8,12},{12,16},{16,20},{20,24},{24,28},{1,5},{5,9},{9,... | collective-permute-start | bytes 393224 | tf_op jit(solution)/shard_map/while/body/eval_jaxpr/ppermute | solution.py:22
  101.2 26.3 %copy-start.4 = (bf16[256,768]{1,0:T(8,128)(2,1)S(1)}, bf16[256,768]{1,0:T(8,128)(2,1)}, u32[]{:S(2)}) copy-start(bf16[256,768]{1,0:T(8,128)(2,1)} %param.11) | copy-start | bytes 1179652
  (11 other events, 14.2 us)
Sparse Core Ops, SparseCore 0:
  103.4 15.8 all-gather.3
